TPU v7x, 256 devices: a whole 4x4x8 slice. The times are simulated.
256 devices in a mesh: dp: 8 (over y, x_hi), shard: 32 (over x_lo, z, core).
Axes of the slice: x: 4 (x_hi: 2, x_lo: 2; x = x_hi * 2 + x_lo), y: 4, z: 8, core: 2. Of those that a mesh axis runs over, the one named last changes fastest.
Arguments:
- grads: float32 [8, 1, 2, 4096, 4096], P('dp', None, None, None, 'shard'), may hold values from -6 to 6
- params: float32 [1, 2, 4096, 4096], P(None, None, ('dp', 'shard')), may hold values from -0.09375 to 0.09375
- moment_one: float32 [1, 2, 4096, 4096], P(None, None, ('dp', 'shard')), may hold values from -0.75 to 0.75
- moment_two: float32 [1, 2, 4096, 4096], P(None, None, ('dp', 'shard')), may hold values from 1e-05 to 0.01
- relation_ids: int32 [1], replicated, may hold values from 0 to 63
- rates: float32 [64], replicated, may hold values from 0.02 to 0.1
- step_count: int32 [1], replicated, may hold values from 1 to 8
Outputs:
- new_params: float32 [1, 2, 4096, 4096], P(None, None, ('dp', 'shard'))
- new_moment_one: float32 [1, 2, 4096, 4096], P(None, None, ('dp', 'shard'))
- new_moment_two: float32 [1, 2, 4096, 4096], P(None, None, ('dp', 'shard'))
- panels: bfloat16 [1, 2, 4096, 4096], P(None, None, None, 'shard')
Inputs may be any that keep to these rules, and one draw needn't show every extreme that they name: `relation_ids`: relation ids are edge types. `step_count`: the step count is positive.
All inputs are finite; a program needn't handle non-finite values.
Results may differ from a plain program's by a relative error of at most 0.001.
Values may be sent and summed in bfloat16 or wider, within the bound.
No kernel may reach another device: no remote copies, remote signals or barrier semaphores. Data moves between devices by JAX's collectives and lax.ppermute only.
A program may use at most 128 MiB of HBM per device.

v0:
```python
import jax
import jax.numpy as jnp
from jax import lax
from jax.sharding import PartitionSpec as P


def body(grads, params, moment_one, moment_two, relation_ids, rates, step_count):
    groups = lax.axis_size("dp")
    owners = lax.axis_size("shard")
    relations = grads.shape[1]
    rows = grads.shape[3]
    panel_cols = grads.shape[-1]
    width = panel_cols * owners
    owned = params.shape[2]
    block = rows // groups
    summed = lax.psum_scatter(grads[0], "dp", scatter_dimension=2, tiled=True)
    pieces = summed.reshape(relations, 2, owners, owned, panel_cols)
    moved = lax.all_to_all(pieces, "shard", split_axis=2, concat_axis=2, tiled=True)
    gradient = moved.transpose(0, 1, 3, 2, 4).reshape(relations, 2, owned, width) / groups
    onehot = (relation_ids[:, None] == jnp.arange(rates.shape[0], dtype=jnp.int32)[None, :]).astype(
        jnp.float32
    )
    learn = jnp.sum(onehot * rates[None, :], axis=1)[:, None, None, None]
    new_one = 0.9 * moment_one + 0.1 * gradient
    new_two = 0.95 * moment_two + 0.05 * gradient * gradient
    steps = step_count[0].astype(jnp.float32)
    fix_one = 1.0 - jnp.power(jnp.float32(0.9), steps)
    fix_two = 1.0 - jnp.power(jnp.float32(0.95), steps)
    update = new_one / fix_one / (jnp.sqrt(new_two / fix_two) + 1e-08) + 0.1 * params
    new_params = params - learn * update
    fresh = new_params.astype(jnp.bfloat16).reshape(relations, 2, owned, owners, panel_cols)
    fresh = fresh.transpose(0, 1, 3, 2, 4)
    back = lax.all_to_all(fresh, "shard", split_axis=2, concat_axis=2, tiled=True)
    back = back.reshape(relations, 2, block, panel_cols)
    panels = lax.all_gather(back, "dp", axis=2, tiled=True)
    return (new_params, new_one, new_two, panels)


def solution(mesh):
    in_specs = (
        P("dp", None, None, None, "shard"),
        P(None, None, ("dp", "shard"), None),
        P(None, None, ("dp", "shard"), None),
        P(None, None, ("dp", "shard"), None),
        P(),
        P(),
        P(),
    )
    out_specs = (
        P(None, None, ("dp", "shard"), None),
        P(None, None, ("dp", "shard"), None),
        P(None, None, ("dp", "shard"), None),
        P(None, None, None, "shard"),
    )
    return jax.shard_map(body, mesh=mesh, in_specs=in_specs, out_specs=out_specs, check_vma=False)
```

profile of v0, /device:TPU:1, one launch (start us, length us, event | category | flops | bytes accessed | tf_op | source)
XLA Modules:
  0.0 216.3 jit_solution(13947312932788557129)
XLA Ops:
  7.2 0.0 reduce-scatter.2.cloned.1.call-start
  7.2 0.7 reduce-scatter.2.cloned.1.call-update
  7.9 0.0 copy-start.3
  7.9 0.0 copy-start
  7.9 0.0 copy-start.1
  7.9 0.0 copy-start.2
  7.9 96.5 %reduce-scatter.2.cloned.1.call-done = f32[1,2,512,128]{3,2,1,0:T(8,128)} async-done(((f32[1,2,4096,128]{3,2,1,0:T(8,128)}), f32[1,2,512,128]{3,2,1,0:T(8,128)}) %reduce-scatter.2.cloned.1.call-update) | async-done | bytes 524304 | tf_op jit(solution)/shard_map/reduce_scatter | solution.py:16
  104.5 1.9 copy.29
  106.4 9.3 %all-to-all-start = ((f32[1,2,32,16,128]{4,3,1,0,2:T(8,128)}), f32[1,2,32,16,128]{4,3,1,0,2:T(8,128)S(1)}, u32[]{:S(2)}, u32[]{:S(2)}) async-start(f32[1,2,32,16,128]{4,3,1,0,2:T(8,128)} %copy.29), calls=%async_computation.1 | async-start | bytes 1048576 | tf_op jit(solution)/shard_map/all_to_all | solution.py:18
  115.7 0.0 all-gather.2.cloned.1.call-start
  117.1 0.0 copy-done.3
  117.1 0.7 fusion
  117.8 14.5 %all-to-all-done = f32[1,2,32,16,128]{4,3,1,0,2:T(8,128)S(1)} async-done(((f32[1,2,32,16,128]{4,3,1,0,2:T(8,128)}), f32[1,2,32,16,128]{4,3,1,0,2:T(8,128)S(1)}, u32[]{:S(2)}, u32[]{:S(2)}) %all-to-all-start) | async-done | bytes 524320 | tf_op jit(solution)/shard_map/all_to_all | solution.py:18
  132.3 0.4 copy_multiply_fusion
  132.6 0.0 copy-done
  132.6 0.0 copy-done.1
  132.7 0.0 copy-done.2
  132.7 2.5 %fusion.1 = (bf16[1,2,16,4096]{3,2,1,0:T(8,128)(2,1)S(1)}, f32[1,2,16,4096]{3,2,1,0:T(8,128)}, f32[1,2,16,4096]{3,2,1,0:T(8,128)}, f32[1,2,16,4096]{3,2,1,0:T(8,128)}) fusion(f32[1,2,16,4096]{3,2,1,0:T(8,128)S(1)} %copy-done, f32[]{:T(128)} %bitcast.8, f32[]{:T(128)} %bitcast.5, f32[]{:T(128)} %fusion, f32[1,2,16,4096]{3,0,2,1:T(1,128)S(1)} %bitcast.22, ...), kind=kLoop, calls=%fused_computation.7 | loop fusion | flops 1703936 | bytes 4456460 | tf_op jit(solution)/shard_map/convert_element_type | solution.py:31
  135.3 0.1 copy.35
  135.4 16.6 %all_to_all.10 = bf16[1,2,32,16,128]{4,3,1,0,2:T(8,128)(2,1)S(1)} all-to-all(bf16[1,2,32,16,128]{4,3,1,0,2:T(8,128)(2,1)S(1)} %copy.35), channel_id=1, replica_groups=mesh['dp'=8,'shard'=32] {'shard'}, dimensions={2} | all-to-all | bytes 524288 | tf_op jit(solution)/shard_map/all_to_all | solution.py:33
  152.0 0.7 copy.36
  152.7 0.0 all-gather.2.cloned.1.call-update
  152.7 53.7 %all-gather.2.cloned.1.call-done = bf16[1,2,4096,128]{3,2,1,0:T(8,128)(2,1)} async-done(((bf16[1,2,512,128]{3,2,1,0:T(8,128)(2,1)}), bf16[1,2,4096,128]{3,2,1,0:T(8,128)(2,1)}) %all-gather.2.cloned.1.call-update) | async-done | bytes 2097168 | tf_op jit(solution)/shard_map/all_gather | solution.py:35
  206.4 3.0 %copy.47 = bf16[1,2,4096,128]{3,2,1,0:T(8,128)(2,1)} copy(bf16[1,2,4096,128]{3,2,1,0:T(8,128)(2,1)} %all-gather.2.cloned.1.call-done) | data formatting | bytes 4194304
  (1 shorter events, 0.0 us)
Async XLA Ops:
  7.2 97.3 %reduce-scatter.2.cloned.1.call-start = ((), (), s32[]{:S(2)}) async-start(), calls=%async_computation.3 | async-start | bytes 4718592 | tf_op jit(solution)/shard_map/reduce_scatter | solution.py:16
  7.9 109.2 %copy-start.3 = (f32[64]{0:T(128)S(1)}, f32[64]{0:T(128)}, u32[]{:S(2)}) copy-start(f32[64]{0:T(128)} %param.12) | copy-start | bytes 772
  7.9 124.7 %copy-start = (f32[1,2,16,4096]{3,2,1,0:T(8,128)S(1)}, f32[1,2,16,4096]{3,2,1,0:T(8,128)}, u32[]{:S(2)}) copy-start(f32[1,2,16,4096]{3,2,1,0:T(8,128)} %param.8) | copy-start | bytes 1572868
  7.9 124.7 %copy-start.1 = (f32[1,2,16,4096]{3,2,1,0:T(8,128)S(1)}, f32[1,2,16,4096]{3,2,1,0:T(8,128)}, u32[]{:S(2)}) copy-start(f32[1,2,16,4096]{3,2,1,0:T(8,128)} %param.10) | copy-start | bytes 1572868
  7.9 124.7 %copy-start.2 = (f32[1,2,16,4096]{3,2,1,0:T(8,128)S(1)}, f32[1,2,16,4096]{3,2,1,0:T(8,128)}, u32[]{:S(2)}) copy-start(f32[1,2,16,4096]{3,2,1,0:T(8,128)} %param.9) | copy-start | bytes 1572868
  106.4 25.9 %all-to-all-start = ((f32[1,2,32,16,128]{4,3,1,0,2:T(8,128)}), f32[1,2,32,16,128]{4,3,1,0,2:T(8,128)S(1)}, u32[]{:S(2)}, u32[]{:S(2)}) async-start(f32[1,2,32,16,128]{4,3,1,0,2:T(8,128)} %copy.29), calls=%async_computation.1 | async-start | bytes 1048576 | tf_op jit(solution)/shard_map/all_to_all | solution.py:18
  115.7 90.8 %all-gather.2.cloned.1.call-start = ((), (), s32[]{:S(2)}) async-start(), calls=%async_computation.4 | async-start | bytes 2359296 | tf_op jit(solution)/shard_map/all_gather | solution.py:35
Sparse Core Ops, SparseCore 0:
  12.1 92.3 reduce-scatter.1
  152.8 53.5 all-gather.1
where the time goes:
time: 217 us; the launch traced here: 216 us
  waiting for transfers between devices  165 us (76%)
  blocking collectives  16.6 us (8%)
  between operations  15.5 us (7%)
  starting transfers between devices  9.35 us (4%)
  local copies, waits for them, and re-layouts  5.83 us (3%)
  other arithmetic  3.57 us (2%)
    reduce_scatter x1, waiting for transfers between devices, body(): summed = lax.psum_scatter(grads[0], 'dp', scatter_dimension=2, tiled=True)  96.5 us
    all_gather x1, waiting for transfers between devices, body(): panels = lax.all_gather(back, 'dp', axis=2, tiled=True)  53.7 us
    all_to_all x1, blocking collectives, body(): lax.all_to_all(fresh, 'shard', split_axis=2, concat_axis=2, tiled=True)  16.6 us
    all_to_all x1, waiting for transfers between devices, body(): lax.all_to_all(pieces, 'shard', split_axis=2, concat_axis=2, tiled=True)  14.5 us
    all_to_all x1, starting transfers between devices, body(): lax.all_to_all(pieces, 'shard', split_axis=2, concat_axis=2, tiled=True)  9.27 us
  transfers between devices with their start and end apart: 3, of which 3 were waited for; matrix products, arithmetic and copies ran while one was open for 0% of the time, Pallas kernels for 0%

commit v1 on v0

--- a/solution.py
+++ b/solution.py
@@ -32,7 +32,9 @@
     fresh = fresh.transpose(0, 1, 3, 2, 4)
     back = lax.all_to_all(fresh, "shard", split_axis=2, concat_axis=2, tiled=True)
     back = back.reshape(relations, 2, block, panel_cols)
-    panels = lax.all_gather(back, "dp", axis=2, tiled=True)
+    panels = jnp.concatenate(
+        lax.all_to_all(jnp.stack([back] * lax.axis_size("dp")), "dp", 0, 0), axis=2
+    )
     return (new_params, new_one, new_two, panels)
 
 

time: 217 us -> 193 us (0.89)
  waiting for transfers between devices: 165 us -> 112 us
  blocking collectives: 16.6 us -> 47.7 us
    all_gather x1 -> x0, waiting for transfers between devices: 53.7 us -> none  [body(): panels = lax.all_gather(back, 'dp', axis=2, tiled=True)]
    all_to_all x0 -> x1, blocking collectives: none -> 31.1 us  [body(): lax.all_to_all(jnp.stack([back] * lax.axis_size('dp')), 'dp', 0, 0)]
    unnamed x10 -> x9, local copies, waits for them, and re-layouts: 3.1 us -> 0.06 us
  transfers between devices with their start and end apart: 3 -> 2, of which waited for: 3 -> 2; matrix products, arithmetic and copies ran while one was open for 0% -> 0% of each run, Pallas kernels for 0% -> 0%
where the time goes in v1:
time: 193 us; the launch traced here: 192 us
  waiting for transfers between devices  112 us (58%)
  blocking collectives  47.7 us (25%)
  between operations  15.5 us (8%)
  starting transfers between devices  9.31 us (5%)
  local copies, waits for them, and re-layouts  3.95 us (2%)
  other arithmetic  3.66 us (2%)
    reduce_scatter x1, waiting for transfers between devices, body(): summed = lax.psum_scatter(grads[0], 'dp', scatter_dimension=2, tiled=True)  96.5 us
    all_to_all x1, blocking collectives, body(): lax.all_to_all(jnp.stack([back] * lax.axis_size('dp')), 'dp', 0, 0)  31.1 us
    all_to_all x1, blocking collectives, body(): lax.all_to_all(fresh, 'shard', split_axis=2, concat_axis=2, tiled=True)  16.6 us
    all_to_all x1, waiting for transfers between devices, body(): lax.all_to_all(pieces, 'shard', split_axis=2, concat_axis=2, tiled=True)  14.5 us
    all_to_all x1, starting transfers between devices, body(): lax.all_to_all(pieces, 'shard', split_axis=2, concat_axis=2, tiled=True)  9.27 us
  transfers between devices with their start and end apart: 2, of which 2 were waited for; matrix products, arithmetic and copies ran while one was open for 0% of the time, Pallas kernels for 0%

profile of v1, /device:TPU:1, one launch (start us, length us, event | category | flops | bytes accessed | tf_op | source)
XLA Modules:
  0.0 191.9 jit_solution(574999542562406544)
XLA Ops:
  7.2 0.0 reduce-scatter.2.cloned.1.call-start
  7.2 0.7 reduce-scatter.2.cloned.1.call-update
  7.9 0.0 copy-start.3
  7.9 0.0 copy-start
  7.9 0.0 copy-start.1
  7.9 0.0 copy-start.2
  7.9 96.5 %reduce-scatter.2.cloned.1.call-done = f32[1,2,512,128]{3,2,1,0:T(8,128)} async-done(((f32[1,2,4096,128]{3,2,1,0:T(8,128)}), f32[1,2,512,128]{3,2,1,0:T(8,128)}) %reduce-scatter.2.cloned.1.call-update) | async-done | bytes 524304 | tf_op jit(solution)/shard_map/reduce_scatter | solution.py:16
  104.5 1.9 copy.34
  106.4 9.3 %all-to-all-start = ((f32[1,2,32,16,128]{4,3,1,0,2:T(8,128)}), f32[1,2,32,16,128]{4,3,1,0,2:T(8,128)S(1)}, u32[]{:S(2)}, u32[]{:S(2)}) async-start(f32[1,2,32,16,128]{4,3,1,0,2:T(8,128)} %copy.34), calls=%async_computation.1 | async-start | bytes 1048576 | tf_op jit(solution)/shard_map/all_to_all | solution.py:18
  117.1 0.0 copy-done.3
  117.1 0.7 fusion
  117.7 14.5 %all-to-all-done = f32[1,2,32,16,128]{4,3,1,0,2:T(8,128)S(1)} async-done(((f32[1,2,32,16,128]{4,3,1,0,2:T(8,128)}), f32[1,2,32,16,128]{4,3,1,0,2:T(8,128)S(1)}, u32[]{:S(2)}, u32[]{:S(2)}) %all-to-all-start) | async-done | bytes 524320 | tf_op jit(solution)/shard_map/all_to_all | solution.py:18
  132.3 0.4 copy_multiply_fusion
  132.6 0.0 copy-done
  132.6 0.0 copy-done.1
  132.7 0.0 copy-done.2
  132.7 2.6 %fusion.1 = (bf16[1,2,16,4096]{3,2,1,0:T(8,128)(2,1)S(1)}, f32[1,2,16,4096]{3,2,1,0:T(8,128)}, f32[1,2,16,4096]{3,2,1,0:T(8,128)}, f32[1,2,16,4096]{3,2,1,0:T(8,128)}) fusion(f32[1,2,16,4096]{3,2,1,0:T(8,128)S(1)} %copy-done, f32[]{:T(128)} %bitcast.8, f32[]{:T(128)} %bitcast.5, f32[]{:T(128)} %fusion, f32[1,2,16,4096]{3,0,2,1:T(1,128)S(1)} %bitcast.26, ...), kind=kLoop, calls=%fused_computation.7 | loop fusion | flops 1703936 | bytes 4456460 | tf_op jit(solution)/shard_map/convert_element_type | solution.py:31
  135.3 0.1 copy.40
  135.4 16.6 %all_to_all.15 = bf16[1,2,32,16,128]{4,3,1,0,2:T(8,128)(2,1)S(1)} all-to-all(bf16[1,2,32,16,128]{4,3,1,0,2:T(8,128)(2,1)S(1)} %copy.40), channel_id=1, replica_groups=mesh['dp'=8,'shard'=32] {'shard'}, dimensions={2} | all-to-all | bytes 524288 | tf_op jit(solution)/shard_map/all_to_all | solution.py:33
  152.1 0.4 stack.3
  152.5 31.1 %all_to_all.16 = bf16[8,1,2,512,128]{4,3,2,1,0:T(8,128)(2,1)S(1)} all-to-all(bf16[8,1,2,512,128]{4,3,2,1,0:T(8,128)(2,1)S(1)} %stack.3), channel_id=1, replica_groups=mesh['dp'=8,'shard'=32] {'dp'}, dimensions={0} | all-to-all | bytes 4194304 | tf_op jit(solution)/shard_map/all_to_all | solution.py:36
  183.5 1.5 copy.42
  (2 shorter events, 0.1 us)
Async XLA Ops:
  7.2 97.3 %reduce-scatter.2.cloned.1.call-start = ((), (), s32[]{:S(2)}) async-start(), calls=%async_computation.4 | async-start | bytes 4718592 | tf_op jit(solution)/shard_map/reduce_scatter | solution.py:16
  7.9 109.2 %copy-start.3 = (f32[64]{0:T(128)S(1)}, f32[64]{0:T(128)}, u32[]{:S(2)}) copy-start(f32[64]{0:T(128)} %param.12) | copy-start | bytes 772
  7.9 124.7 %copy-start = (f32[1,2,16,4096]{3,2,1,0:T(8,128)S(1)}, f32[1,2,16,4096]{3,2,1,0:T(8,128)}, u32[]{:S(2)}) copy-start(f32[1,2,16,4096]{3,2,1,0:T(8,128)} %param.8) | copy-start | bytes 1572868
  7.9 124.7 %copy-start.1 = (f32[1,2,16,4096]{3,2,1,0:T(8,128)S(1)}, f32[1,2,16,4096]{3,2,1,0:T(8,128)}, u32[]{:S(2)}) copy-start(f32[1,2,16,4096]{3,2,1,0:T(8,128)} %param.10) | copy-start | bytes 1572868
  7.9 124.7 %copy-start.2 = (f32[1,2,16,4096]{3,2,1,0:T(8,128)S(1)}, f32[1,2,16,4096]{3,2,1,0:T(8,128)}, u32[]{:S(2)}) copy-start(f32[1,2,16,4096]{3,2,1,0:T(8,128)} %param.9) | copy-start | bytes 1572868
  106.4 25.9 %all-to-all-start = ((f32[1,2,32,16,128]{4,3,1,0,2:T(8,128)}), f32[1,2,32,16,128]{4,3,1,0,2:T(8,128)S(1)}, u32[]{:S(2)}, u32[]{:S(2)}) async-start(f32[1,2,32,16,128]{4,3,1,0,2:T(8,128)} %copy.34), calls=%async_computation.1 | async-start | bytes 1048576 | tf_op jit(solution)/shard_map/all_to_all | solution.py:18
Sparse Core Ops, SparseCore 0:
  12.1 92.3 reduce-scatter.1
